TPU v7x, 256 devices: a whole 4x4x8 slice. The times are simulated.
256 devices in a mesh: req: 8 (over x, z_hi), blk: 32 (over y, z_lo, core).
Axes of the slice: x: 4, y: 4, z: 8 (z_hi: 2, z_lo: 4; z = z_hi * 4 + z_lo), core: 2. Of those that a mesh axis runs over, the one named last changes fastest.
Arguments:
- tokens: bfloat16 [256, 128, 1536], P(('req', 'blk')), may hold values from -6 to 6
- cache_kv: bfloat16 [256, 2, 256, 384], P(('req', 'blk')), may hold values from -200 to 200
- cache_len: int32 [256], P(('req', 'blk')), may hold values from 2 to 256, as said below
- holder: int32 [256], P(('req', 'blk')), may hold values from 0 to 7, as said below
- accept: int32 [256, 128], P(('req', 'blk')), may hold values from 0 to 1, as said below
- attn_gain: float32 [1536], replicated, may hold values from 0.1 to 1.9
- q_weight: bfloat16 [1536, 768], replicated, may hold values from -0.15625 to 0.15625
- k_weight: bfloat16 [1536, 384], replicated, may hold values from -0.15625 to 0.15625
- v_weight: bfloat16 [1536, 384], replicated, may hold values from -0.15625 to 0.15625
- o_weight: bfloat16 [768, 1536], replicated, may hold values from -0.21875 to 0.21875
- ffn_gain: float32 [1536], replicated, may hold values from 0.4 to 2.5
- w_gate: bfloat16 [1536, 4096], P(None, 'blk'), may hold values from -0.15625 to 0.15625
- w_up: bfloat16 [1536, 4096], P(None, 'blk'), may hold values from -0.15625 to 0.15625
- w_down: bfloat16 [4096, 1536], P('blk'), may hold values from -0.09375 to 0.09375
Outputs:
- refined: float32 [256, 128, 1536], P(('req', 'blk'))
Inputs may be any that keep to these rules, and one draw needn't show every extreme that they name: `holder`: requests whose numbers agree modulo 32 have distinct holders. `cache_len`: some request has exactly 256 cached positions. `accept`: each request accepts exactly 64 positions.
All inputs are finite; a program needn't handle non-finite values.
Results may differ from a plain program's by a relative error of at most 0.04.
Values may be sent and summed in bfloat16 or wider, within the bound.
No kernel may reach another device: no remote copies, remote signals or barrier semaphores. Data moves between devices by JAX's collectives and lax.ppermute only.
A program may use at most 128 MiB of HBM per device.

v0:
```python
import jax
import jax.numpy as jnp
from jax import lax
from jax.sharding import PartitionSpec as P

HEAD = 96
norm_eps = 1e-05
rope_base = 100000.0


def rms_scale(values, gain_row):
    return (
        values * lax.rsqrt(jnp.mean(values * values, axis=-1, keepdims=True) + norm_eps) * gain_row
    )


def rotate_heads(flat, positions, head_count):
    half_dim = HEAD // 2
    shaped = flat.reshape(flat.shape[0], head_count, HEAD)
    freqs = jnp.exp(-jnp.log(rope_base) * 2.0 * jnp.arange(half_dim, dtype=jnp.float32) / HEAD)
    angles = positions[:, None] * freqs[None, :]
    cosine = jnp.cos(angles)[:, None, :]
    sine = jnp.sin(angles)[:, None, :]
    first_half = shaped[..., :half_dim]
    second_half = shaped[..., half_dim:]
    turned = jnp.concatenate(
        [first_half * cosine - second_half * sine, second_half * cosine + first_half * sine],
        axis=-1,
    )
    return turned.reshape(flat.shape[0], head_count * HEAD)


def attend_block(
    tok_rows,
    cache_keys,
    cache_vals,
    cache_length,
    attn_gain,
    q_weight,
    k_weight,
    v_weight,
    o_weight,
):
    block_len = tok_rows.shape[0]
    slot_len = cache_keys.shape[0]
    kv_count = k_weight.shape[1] // HEAD
    q_count = q_weight.shape[1] // HEAD
    widened = tok_rows.astype(jnp.float32)
    normed = rms_scale(widened, attn_gain).astype(jnp.bfloat16)
    positions = (cache_length + jnp.arange(block_len, dtype=jnp.int32)).astype(jnp.float32)
    queries = rotate_heads(
        jnp.dot(normed, q_weight, preferred_element_type=jnp.float32), positions, q_count
    ).astype(jnp.bfloat16)
    new_keys = rotate_heads(
        jnp.dot(normed, k_weight, preferred_element_type=jnp.float32), positions, kv_count
    ).astype(jnp.bfloat16)
    new_vals = jnp.dot(normed, v_weight, preferred_element_type=jnp.float32).astype(jnp.bfloat16)
    all_keys = jnp.concatenate([cache_keys, new_keys], axis=0).reshape(
        slot_len + block_len, kv_count, HEAD
    )
    all_vals = jnp.concatenate([cache_vals, new_vals], axis=0).reshape(
        slot_len + block_len, kv_count, HEAD
    )
    grouped = queries.reshape(block_len, kv_count, q_count // kv_count, HEAD)
    scores = jnp.einsum(
        "bgid,kgd->gibk", grouped, all_keys, preferred_element_type=jnp.float32
    ) * HEAD ** (-0.5)
    valid = jnp.concatenate(
        [
            jnp.arange(slot_len, dtype=jnp.int32) < cache_length,
            jnp.ones((block_len,), dtype=jnp.bool_),
        ]
    )
    scores = jnp.where(valid, scores, -jnp.inf)
    peaks = jnp.max(scores, axis=-1, keepdims=True)
    expd = jnp.exp(scores - peaks)
    probs = (expd / jnp.sum(expd, axis=-1, keepdims=True)).astype(jnp.bfloat16)
    context = jnp.einsum("gibk,kgd->bgid", probs, all_vals, preferred_element_type=jnp.float32)
    context = context.astype(jnp.bfloat16).reshape(block_len, q_count * HEAD)
    return widened + jnp.dot(context, o_weight, preferred_element_type=jnp.float32)


def run_ffn(normed_rows, w_gate, w_up, w_down, down_all):
    part_rows = lax.all_gather(normed_rows, "blk", axis=0, tiled=True)
    gate_vals = jnp.dot(part_rows, w_gate, preferred_element_type=jnp.float32)
    up_vals = jnp.dot(part_rows, w_up, preferred_element_type=jnp.float32)
    hidden_all = (jax.nn.silu(gate_vals) * up_vals).astype(jnp.bfloat16)
    hidden_own = lax.all_to_all(hidden_all, "blk", 0, 1, tiled=True)
    groups = w_down.shape[0]
    group_count = down_all.shape[0] // groups
    terms = jnp.einsum(
        "rgk,gkd->grd",
        hidden_own.reshape(hidden_own.shape[0], group_count, groups),
        down_all.reshape(group_count, groups, down_all.shape[1]),
        preferred_element_type=jnp.float32,
    ).astype(jnp.bfloat16)
    return jnp.sum(terms.astype(jnp.float32), axis=0)


def fetch_slot(cache_kv, holder):
    count = lax.axis_size("req")
    own = cache_kv[0]
    if count != 8:
        slots = lax.all_gather(own, "req", axis=0, tiled=False)
        return slots[holder[0]]
    me = lax.axis_index("req")

    def swap(values, mask):
        return lax.ppermute(values, "req", perm=[(i, i ^ mask) for i in range(count)])

    def pick(cond, a, b):
        return jnp.where(cond, a, b)

    near = swap(holder, 1)
    quad = swap(jnp.concatenate([holder, near]), 2)
    holders = {0: holder[0], 1: near[0], 2: quad[0], 3: quad[1]}
    got1 = swap(own, 4)
    send_a = pick(holders[2] == me ^ 4, got1, own)
    send_b = pick(holders[3] == me ^ 4, got1, own)
    got2 = swap(jnp.stack([send_a, send_b]), 2)
    want = holders[1]
    send_c = pick(want == me, own, pick(want == me ^ 4, got1, got2[1]))
    got3 = swap(send_c, 1)
    need = holders[0]
    return pick(
        need == me,
        own,
        pick(
            need == me ^ 4, got1, pick(need ^ me == 2, got2[0], pick(need ^ me == 6, got2[0], got3))
        ),
    )


def local(
    tokens,
    cache_kv,
    cache_len,
    holder,
    accept,
    attn_gain,
    q_weight,
    k_weight,
    v_weight,
    o_weight,
    ffn_gain,
    w_gate,
    w_up,
    w_down,
):
    fetched = fetch_slot(cache_kv, holder)
    copies = jnp.broadcast_to(w_down[None], (lax.axis_size("blk"),) + w_down.shape)
    down_all = lax.all_to_all(copies, "blk", 0, 0, tiled=True).reshape(-1, w_down.shape[1])
    fetched, down_all = lax.optimization_barrier((fetched, down_all))
    cache_keys = fetched[0]
    cache_vals = fetched[1]
    cache_length = cache_len[0]
    block_rows = tokens[0]
    first_pass = attend_block(
        block_rows,
        cache_keys,
        cache_vals,
        cache_length,
        attn_gain,
        q_weight,
        k_weight,
        v_weight,
        o_weight,
    )
    chosen_mask = accept[0] == 1
    ffn_sum = run_ffn(
        rms_scale(first_pass, ffn_gain).astype(jnp.bfloat16), w_gate, w_up, w_down, down_all
    )
    placed = first_pass + ffn_sum
    second_in = jnp.where(chosen_mask[:, None], placed, block_rows.astype(jnp.float32))
    refined = attend_block(
        second_in,
        cache_keys,
        cache_vals,
        cache_length,
        attn_gain,
        q_weight,
        k_weight,
        v_weight,
        o_weight,
    )
    return refined[None]


def solution(mesh):
    return jax.shard_map(
        local,
        mesh=mesh,
        in_specs=(
            P(("req", "blk"), None, None),
            P(("req", "blk"), None, None, None),
            P(("req", "blk")),
            P(("req", "blk")),
            P(("req", "blk"), None),
            P(),
            P(),
            P(),
            P(),
            P(),
            P(),
            P(None, "blk"),
            P(None, "blk"),
            P("blk", None),
        ),
        out_specs=P(("req", "blk"), None, None),
        check_vma=False,
    )
```

profile of v0, /device:TPU:1, one launch (start us, length us, event | category | flops | bytes accessed | tf_op | source)
XLA Modules:
  0.0 477.4 jit_solution(10398602093591844268)
XLA Ops:
  6.5 7.1 %broadcast_in_dim.20 = bf16[32,128,1536]{2,1,0:T(8,128)(2,1)} broadcast(bf16[128,1536]{1,0:T(8,128)(2,1)} %param.27), dimensions={1,2} | broadcast | bytes 12976128 | tf_op jit(solution)/shard_map/broadcast_in_dim | solution.py:151
  13.6 10.4 %all-to-all-start = ((bf16[32,128,1536]{2,1,0:T(8,128)(2,1)}), bf16[32,128,1536]{2,1,0:T(8,128)(2,1)}, u32[]{:S(2)}, u32[]{:S(2)}) async-start(bf16[32,128,1536]{2,1,0:T(8,128)(2,1)} %broadcast_in_dim.20), calls=%async_computation | async-start | bytes 25165824 | tf_op jit(solution)/shard_map/all_to_all | solution.py:152
  24.0 0.0 all-gather.2.cloned.1.call-start
  24.0 2.8 collective-permute-start
  26.9 4.2 collective-permute-start.1
  31.8 0.0 copy-start.2
  31.8 4.4 copy.29
  36.8 0.2 fusion.18
  37.0 3.3 fusion.55
  40.3 0.5 add_convert_fusion.4
  40.8 200.4 %collective-permute-done.1 = s32[1]{0:T(128)} collective-permute-done((s32[1]{0:T(128)}, s32[1]{0:T(128)}, u32[]{:S(2)}, u32[]{:S(2)}) %collective-permute-start.1) | collective-permute-done | bytes 36 | tf_op jit(solution)/shard_map/ppermute | solution.py:109
  241.3 0.7 pad_add_fusion
  242.0 1.2 collective-permute-start.2
  243.2 1.6 collective-permute-done.2
  244.8 0.6 fusion.77
  246.7 0.1 select_bitcast_fusion.1
  246.8 1.0 pad_maximum_fusion
  247.8 1.2 collective-permute-start.3
  249.0 0.8 multiply_cosine_fusion
  249.8 2.5 copy.28
  252.3 1.9 subtract_convert_fusion.1
  254.1 2.3 convolution_convert_fusion.4
  256.5 1.2 fusion.57
  259.0 6.3 %collective-permute-done.3 = bf16[2,2,256,384]{3,2,1,0:T(8,128)(2,1)} collective-permute-done((bf16[2,2,256,384]{3,2,1,0:T(8,128)(2,1)}, bf16[2,2,256,384]{3,2,1,0:T(8,128)(2,1)}, u32[]{:S(2)}, u32[]{:S(2)}) %collective-permute-start.3) | collective-permute-done | bytes 786464 | tf_op jit(solution)/shard_map/ppermute | solution.py:109
  265.3 1.8 fusion.28
  267.1 1.2 collective-permute-start.4
  268.3 1.6 copy.26
  269.9 1.6 pad_maximum_fusion.5
  271.5 1.6 subtract_convert_fusion.3
  273.1 6.1 %collective-permute-done.4 = bf16[2,256,384]{2,1,0:T(8,128)(2,1)} collective-permute-done((bf16[2,256,384]{2,1,0:T(8,128)(2,1)}, bf16[2,256,384]{2,1,0:T(8,128)(2,1)}, u32[]{:S(2)}, u32[]{:S(2)}) %collective-permute-start.4) | collective-permute-done | bytes 393248 | tf_op jit(solution)/shard_map/ppermute | solution.py:109
  279.2 1.9 fusion.24
  281.1 34.0 %all-to-all-done = bf16[32,128,1536]{2,1,0:T(8,128)(2,1)} async-done(((bf16[32,128,1536]{2,1,0:T(8,128)(2,1)}), bf16[32,128,1536]{2,1,0:T(8,128)(2,1)}, u32[]{:S(2)}, u32[]{:S(2)}) %all-to-all-start) | async-done | bytes 12582944 | tf_op jit(solution)/shard_map/all_to_all | solution.py:152
  315.1 1.1 fusion.76
  316.2 0.1 copy.27
  316.4 0.1 copy.25
  316.6 2.8 fusion.78
  319.4 1.7 convolution_convert_fusion.2
  321.1 0.0 copy-start.20
  321.1 0.6 multiply_reduce_fusion.1
  321.7 0.9 copy-done.4
  322.6 0.9 multiply_convert_fusion.1
  323.5 0.0 all-gather.2.cloned.1.call-update
  323.6 78.8 %all-gather.2.cloned.1.call-done = bf16[4096,1536]{1,0:T(8,128)(2,1)} async-done(((bf16[128,1536]{1,0:T(8,128)(2,1)}), bf16[4096,1536]{1,0:T(8,128)(2,1)}) %all-gather.2.cloned.1.call-update) | async-done | bytes 12582928 | tf_op jit(solution)/shard_map/all_gather | solution.py:84
  402.4 8.0 %fusion.84 = f32[4096,128]{1,0:T(8,128)S(1)} fusion(bf16[4096,1536]{1,0:T(8,128)(2,1)} %all-gather.2.cloned.1.call-done, bf16[1536,128]{1,0:T(8,128)(2,1)S(1)} %copy-done.12), kind=kOutput, calls=%fused_computation.105 | convolution fusion | flops 1610612736 | bytes 15073280 | tf_op jit(solution)/shard_map/dot_general | solution.py:85
  410.4 0.2 copy-done.1
  410.6 4.6 fusion.2
  415.2 6.9 %all-to-all-start.1 = ((bf16[32,128,128]{2,1,0:T(8,128)(2,1)}), bf16[32,128,128]{2,1,0:T(8,128)(2,1)}, u32[]{:S(2)}, u32[]{:S(2)}) async-start(bf16[32,128,128]{2,1,0:T(8,128)(2,1)} %bitcast.158), calls=%async_computation.1 | async-start | bytes 2097152 | tf_op jit(solution)/shard_map/all_to_all | solution.py:88
  422.1 27.9 %all-to-all-done.1 = bf16[32,128,128]{2,1,0:T(8,128)(2,1)} async-done(((bf16[32,128,128]{2,1,0:T(8,128)(2,1)}), bf16[32,128,128]{2,1,0:T(8,128)(2,1)}, u32[]{:S(2)}, u32[]{:S(2)}) %all-to-all-start.1) | async-done | bytes 1048608 | tf_op jit(solution)/shard_map/all_to_all | solution.py:88
  450.0 8.4 %convert_reduce_fusion = f32[128,1536]{1,0:T(8,128)S(1)} fusion(bf16[32,128,1536]{2,1,0:T(8,128)(2,1)} %bitcast.32, bf16[32,128,128]{2,1,0:T(8,128)(2,1)} %all-to-all-done.1), kind=kOutput, calls=%fused_computation.2 | convolution fusion | flops 1629290496 | bytes 14417920 | tf_op jit(solution)/shard_map/rgk,gkd->grd/dot_general | solution.py:91
  458.4 0.3 multiply_reduce_fusion
  458.7 0.1 multiply_convert_fusion
  458.9 1.2 copy-done.3
  460.0 1.1 fusion.86
  461.1 0.2 copy-done.6
  461.3 0.6 fusion.85
  461.9 0.7 copy-done.9
  462.6 0.4 convolution_convert_fusion.3
  463.0 0.1 subtract_convert_fusion
  463.0 0.7 subtract_convert_fusion.2
  463.7 0.1 copy.31
  463.9 0.7 pad_maximum_fusion.6
  464.6 2.9 fusion.81
  467.5 1.7 convolution_convert_fusion.1
  469.2 1.4 fusion.3
  (49 shorter events, 0.1 us)
Async XLA Ops:
  6.5 314.6 %copy-start = (bf16[768,1536]{1,0:T(8,128)(2,1)S(1)}, bf16[768,1536]{1,0:T(8,128)(2,1)}, u32[]{:S(2)}) copy-start(bf16[768,1536]{1,0:T(8,128)(2,1)} %param.23) | copy-start | bytes 7077892
  13.6 10.4 %copy-start.8 = (bf16[1,2,256,384]{3,2,1,0:T(8,128)(2,1)S(1)}, bf16[1,2,256,384]{3,2,1,0:T(8,128)(2,1)}, u32[]{:S(2)}) copy-start(bf16[1,2,256,384]{3,2,1,0:T(8,128)(2,1)} %param.15) | copy-start | bytes 1179652
  13.6 301.5 %all-to-all-start = ((bf16[32,128,1536]{2,1,0:T(8,128)(2,1)}), bf16[32,128,1536]{2,1,0:T(8,128)(2,1)}, u32[]{:S(2)}, u32[]{:S(2)}) async-start(bf16[32,128,1536]{2,1,0:T(8,128)(2,1)} %broadcast_in_dim.20), calls=%async_computation | async-start | bytes 25165824 | tf_op jit(solution)/shard_map/all_to_all | solution.py:152
  24.0 378.4 %all-gather.2.cloned.1.call-start = ((), (), s32[]{:S(2)}) async-start(), calls=%async_computation.2 | async-start | bytes 12976128 | tf_op jit(solution)/shard_map/all_gather | solution.py:84
  24.0 222.7 %collective-permute-start = (bf16[2,256,384]{2,1,0:T(8,128)(2,1)S(1)}, bf16[2,256,384]{2,1,0:T(8,128)(2,1)S(1)}, u32[]{:S(2)}, u32[]{:S(2)}) collective-permute-start(bf16[2,256,384]{2,1,0:T(8,128)(2,1)S(1)} %bitcast.156), channel_id=1, source_target_pairs={{0,128},{32,160},{64,192},{96,224},{128,0},{160,32},{192,64},{224,... | collective-permute-start | bytes 1179656 | tf_op jit(solution)/shard_map/ppermute | solution.py:109
  26.9 214.4 %collective-permute-start.1 = (s32[1]{0:T(128)}, s32[1]{0:T(128)}, u32[]{:S(2)}, u32[]{:S(2)}) collective-permute-start(s32[1]{0:T(128)} %param.17), channel_id=1, source_target_pairs={{0,32},{32,0},{64,96},{96,64},{128,160},{160,128},{192,224},{224,1... | collective-permute-start | bytes 20 | tf_op jit(solution)/shard_map/ppermute | solution.py:109
  31.8 5.0 %copy-start.2 = (bf16[1,128,1536]{2,1,0:T(8,128)(2,1)S(1)}, bf16[1,128,1536]{2,1,0:T(8,128)(2,1)}, u32[]{:S(2)}) copy-start(bf16[1,128,1536]{2,1,0:T(8,128)(2,1)} %param.14) | copy-start | bytes 1179652
  31.8 5.2 %copy-start.17 = (f32[1536]{0:T(1024)S(1)}, f32[1536]{0:T(1024)}, u32[]{:S(2)}) copy-start(f32[1536]{0:T(1024)} %param.19) | copy-start | bytes 18436
  242.0 2.8 collective-permute-start.2
  246.7 2.3 copy-start.21
  247.8 17.5 %collective-permute-start.3 = (bf16[2,2,256,384]{3,2,1,0:T(8,128)(2,1)}, bf16[2,2,256,384]{3,2,1,0:T(8,128)(2,1)}, u32[]{:S(2)}, u32[]{:S(2)}) collective-permute-start(bf16[2,2,256,384]{3,2,1,0:T(8,128)(2,1)} %pad_maximum_fusion), channel_id=1, source_target_pairs={{0,64},{32,96},{64,0},{96,32},{128,192},{160,224},{192,128},{224,1... | collective-permute-start | bytes 2359304 | tf_op jit(solution)/shard_map/ppermute | solution.py:109
  252.3 4.2 copy-start.7
  267.1 12.1 %collective-permute-start.4 = (bf16[2,256,384]{2,1,0:T(8,128)(2,1)}, bf16[2,256,384]{2,1,0:T(8,128)(2,1)}, u32[]{:S(2)}, u32[]{:S(2)}) collective-permute-start(bf16[2,256,384]{2,1,0:T(8,128)(2,1)} %fusion.28), channel_id=1, source_target_pairs={{0,32},{32,0},{64,96},{96,64},{128,160},{160,128},{192,224},{224,1... | collective-permute-start | bytes 1179656 | tf_op jit(solution)/shard_map/ppermute | solution.py:109
  281.1 35.4 %copy-start.18 = (bf16[128,4,48]{0,2,1:T(8,128)(2,1)S(1)}, bf16[128,4,48]{0,2,1:T(8,128)(2,1)}, u32[]{:S(2)}) copy-start(bf16[128,4,48]{0,2,1:T(8,128)(2,1)} %get-tuple-element.21) | copy-start | bytes 147460
  281.1 35.4 %copy-start.19 = (bf16[128,4,48]{0,2,1:T(8,128)(2,1)S(1)}, bf16[128,4,48]{0,2,1:T(8,128)(2,1)}, u32[]{:S(2)}) copy-start(bf16[128,4,48]{0,2,1:T(8,128)(2,1)} %get-tuple-element.22) | copy-start | bytes 147460
  316.4 3.0 copy-start.15
  316.5 2.9 copy-start.13
  316.5 2.9 copy-start.16
  321.1 1.5 copy-start.20
  321.7 0.9 copy-start.4
  321.7 80.7 %copy-start.12 = (bf16[1536,128]{1,0:T(8,128)(2,1)S(1)}, bf16[1536,128]{1,0:T(8,128)(2,1)}, u32[]{:S(2)}) copy-start(bf16[1536,128]{1,0:T(8,128)(2,1)} %param.25) | copy-start | bytes 1179652
  323.5 86.8 %copy-start.22 = (bf16[1536,128]{1,0:T(8,128)(2,1)S(1)}, bf16[1536,128]{1,0:T(8,128)(2,1)}, u32[]{:S(2)}) copy-start(bf16[1536,128]{1,0:T(8,128)(2,1)} %param.26) | copy-start | bytes 1179652
  402.4 8.2 %copy-start.1 = (bf16[4096,1536]{1,0:T(8,128)(2,1)S(1)}, bf16[4096,1536]{1,0:T(8,128)(2,1)}, u32[]{:S(2)}) copy-start(bf16[4096,1536]{1,0:T(8,128)(2,1)} %all-gather.2.cloned.1.call-done) | copy-start | bytes 37748740
  415.2 6.9 %copy-start.23 = (s32[1,128]{1,0:T(1,128)S(1)}, s32[1,128]{1,0:T(1,128)}, u32[]{:S(2)}) copy-start(s32[1,128]{1,0:T(1,128)} %param.18) | copy-start | bytes 1540
  415.2 34.8 %all-to-all-start.1 = ((bf16[32,128,128]{2,1,0:T(8,128)(2,1)}), bf16[32,128,128]{2,1,0:T(8,128)(2,1)}, u32[]{:S(2)}, u32[]{:S(2)}) async-start(bf16[32,128,128]{2,1,0:T(8,128)(2,1)} %bitcast.158), calls=%async_computation.1 | async-start | bytes 2097152 | tf_op jit(solution)/shard_map/all_to_all | solution.py:88
  449.9 8.4 %copy-start.5 = (f32[128,1536]{1,0:T(8,128)S(1)}, f32[128,1536]{1,0:T(8,128)}, u32[]{:S(2)}) copy-start(f32[128,1536]{1,0:T(8,128)} %copy-done.4) | copy-start | bytes 2359300
  458.4 1.7 copy-start.3
  460.0 1.3 copy-start.6
  461.3 1.3 copy-start.9
  461.3 1.7 copy-start.10
  461.3 1.7 copy-start.11
  464.5 2.9 copy-start.14
Sparse Core Ops, SparseCore 0:
  323.7 78.6 all-gather.1
where the time goes:
time: 478 us; the launch traced here: 477 us
  waiting for transfers between devices  355 us (74%)
  matrix products  40.9 us (9%)
  starting transfers between devices  28 us (6%)
  local copies, waits for them, and re-layouts  20.8 us (4%)
  between operations  17.6 us (4%)
  other arithmetic  14.9 us (3%)
    ppermute x5, waiting for transfers between devices, swap(): lax.ppermute(values, 'req', perm=[(i, i ^ mask) for i in range(count)])  214 us
    all_gather x1, waiting for transfers between devices, run_ffn(): part_rows = lax.all_gather(normed_rows, 'blk', axis=0, tiled=True)  78.8 us
    all_to_all x1, waiting for transfers between devices, local(): lax.all_to_all(copies, 'blk', 0, 0, tiled=True).reshape(-1, w_down.shape[1])  34 us
    all_to_all x1, waiting for transfers between devices, run_ffn(): hidden_own = lax.all_to_all(hidden_all, 'blk', 0, 1, tiled=True)  27.9 us
    ppermute x5, starting transfers between devices, swap(): lax.ppermute(values, 'req', perm=[(i, i ^ mask) for i in range(count)])  10.7 us
    all_to_all x1, starting transfers between devices, local(): lax.all_to_all(copies, 'blk', 0, 0, tiled=True).reshape(-1, w_down.shape[1])  10.4 us
    unnamed x50, local copies, waits for them, and re-layouts  9.99 us
  transfers between devices with their start and end apart: 8, of which 7 were waited for; matrix products, arithmetic and copies ran while one was open for 6% of the time, Pallas kernels for 0%

commit v1 on v0

--- a/solution.py
+++ b/solution.py
@@ -81,7 +81,8 @@
 
 
 def run_ffn(normed_rows, w_gate, w_up, w_down, down_all):
-    part_rows = lax.all_gather(normed_rows, "blk", axis=0, tiled=True)
+    sent = jnp.stack([normed_rows] * lax.axis_size("blk"))
+    part_rows = jnp.concatenate(lax.all_to_all(sent, "blk", 0, 0), axis=0)
     gate_vals = jnp.dot(part_rows, w_gate, preferred_element_type=jnp.float32)
     up_vals = jnp.dot(part_rows, w_up, preferred_element_type=jnp.float32)
     hidden_all = (jax.nn.silu(gate_vals) * up_vals).astype(jnp.bfloat16)

time: 478 us -> 667 us (1.40)
  blocking collectives: 0 us -> 280 us
  waiting for transfers between devices: 355 us -> 276 us
  between operations: 17.6 us -> 4.19 us
  local copies, waits for them, and re-layouts: 20.8 us -> 28 us
    all_to_all x0 -> x1, blocking collectives: none -> 280 us  [run_ffn(): part_rows = jnp.concatenate(lax.all_to_all(sent, 'blk', 0, 0), axis=0)]
    all_gather x1 -> x0, waiting for transfers between devices: 78.8 us -> none  [run_ffn(): part_rows = lax.all_gather(normed_rows, 'blk', axis=0, tiled=True)]
  transfers between devices with their start and end apart: 8 -> 7, of which waited for: 7 -> 6; matrix products, arithmetic and copies ran while one was open for 6% -> 4% of each run, Pallas kernels for 0% -> 0%
where the time goes in v1:
time: 667 us; the launch traced here: 666 us
  blocking collectives  280 us (42%)
  waiting for transfers between devices  276 us (41%)
  matrix products  37.1 us (6%)
  local copies, waits for them, and re-layouts  28 us (4%)
  starting transfers between devices  25.9 us (4%)
  other arithmetic  14.1 us (2%)
    all_to_all x1, blocking collectives, run_ffn(): part_rows = jnp.concatenate(lax.all_to_all(sent, 'blk', 0, 0), axis=0)  280 us
    ppermute x5, waiting for transfers between devices, swap(): lax.ppermute(values, 'req', perm=[(i, i ^ mask) for i in range(count)])  214 us
    all_to_all x1, waiting for transfers between devices, local(): lax.all_to_all(copies, 'blk', 0, 0, tiled=True).reshape(-1, w_down.shape[1])  34.1 us
    all_to_all x1, waiting for transfers between devices, run_ffn(): hidden_own = lax.all_to_all(hidden_all, 'blk', 0, 1, tiled=True)  27.9 us
  transfers between devices with their start and end apart: 7, of which 6 were waited for; matrix products, arithmetic and copies ran while one was open for 4% of the time, Pallas kernels for 0%

profile of v1, /device:TPU:1, one launch (start us, length us, event | category | flops | bytes accessed | tf_op | source)
XLA Modules:
  0.0 666.0 jit_solution(4318577298946778751)
XLA Ops:
  0.0 7.0 %broadcast_in_dim.20 = bf16[32,128,1536]{2,1,0:T(8,128)(2,1)} broadcast(bf16[128,1536]{1,0:T(8,128)(2,1)} %param.27), dimensions={1,2} | broadcast | bytes 12976128 | tf_op jit(solution)/shard_map/broadcast_in_dim | solution.py:152
  7.1 10.4 %all-to-all-start = ((bf16[32,128,1536]{2,1,0:T(8,128)(2,1)}), bf16[32,128,1536]{2,1,0:T(8,128)(2,1)}, u32[]{:S(2)}, u32[]{:S(2)}) async-start(bf16[32,128,1536]{2,1,0:T(8,128)(2,1)} %broadcast_in_dim.20), calls=%async_computation | async-start | bytes 25165824 | tf_op jit(solution)/shard_map/all_to_all | solution.py:153
  17.4 2.8 collective-permute-start
  20.3 4.2 collective-permute-start.1
  25.2 0.0 copy-start.1
  25.2 0.0 copy-start.16
  25.2 4.3 copy.29
  30.2 0.2 fusion.18
  30.4 3.3 fusion.55
  33.7 0.5 add_convert_fusion.4
  34.1 200.6 %collective-permute-done.1 = s32[1]{0:T(128)} collective-permute-done((s32[1]{0:T(128)}, s32[1]{0:T(128)}, u32[]{:S(2)}, u32[]{:S(2)}) %collective-permute-start.1) | collective-permute-done | bytes 36 | tf_op jit(solution)/shard_map/ppermute | solution.py:110
  234.7 0.7 pad_add_fusion
  235.4 1.2 collective-permute-start.2
  236.7 1.6 collective-permute-done.2
  238.2 0.6 fusion.77
  240.1 0.1 select_bitcast_fusion.1
  240.2 1.0 pad_maximum_fusion
  241.2 1.2 collective-permute-start.3
  242.4 0.8 multiply_cosine_fusion
  243.2 2.5 copy.28
  245.7 1.9 subtract_convert_fusion.1
  247.5 2.3 convolution_convert_fusion.4
  249.9 1.2 fusion.57
  252.4 6.3 collective-permute-done.3
  258.6 1.8 fusion.28
  260.4 1.2 collective-permute-start.4
  261.6 1.6 copy.26
  263.3 1.6 pad_maximum_fusion.5
  264.9 1.6 subtract_convert_fusion.3
  266.5 6.0 collective-permute-done.4
  272.6 1.9 fusion.24
  274.5 34.1 %all-to-all-done = bf16[32,128,1536]{2,1,0:T(8,128)(2,1)} async-done(((bf16[32,128,1536]{2,1,0:T(8,128)(2,1)}), bf16[32,128,1536]{2,1,0:T(8,128)(2,1)}, u32[]{:S(2)}, u32[]{:S(2)}) %all-to-all-start) | async-done | bytes 12582944 | tf_op jit(solution)/shard_map/all_to_all | solution.py:153
  308.6 1.1 fusion.76
  309.6 0.1 copy.27
  309.8 0.1 copy.25
  310.0 2.8 fusion.78
  312.9 1.7 convolution_convert_fusion.2
  314.6 0.0 copy-start.19
  314.6 0.6 multiply_reduce_fusion.1
  315.2 0.9 copy-done.3
  316.1 0.1 multiply_convert_fusion.1
  316.2 5.9 stack.11
  322.1 280.3 %all_to_all.26 = bf16[32,128,1536]{2,1,0:T(8,128)(2,1)S(1)} all-to-all(bf16[32,128,1536]{2,1,0:T(8,128)(2,1)} %stack.11), channel_id=1, replica_groups=mesh['req'=8,'blk'=32] {'blk'}, dimensions={0} | all-to-all | bytes 25165824 | tf_op jit(solution)/shard_map/all_to_all | solution.py:85
  602.4 3.5 fusion.84
  605.9 4.6 fusion.2
  610.5 4.8 all-to-all-start.2
  615.3 27.9 %all-to-all-done.2 = bf16[32,128,128]{2,1,0:T(8,128)(2,1)} async-done(((bf16[32,128,128]{2,1,0:T(8,128)(2,1)}), bf16[32,128,128]{2,1,0:T(8,128)(2,1)}, u32[]{:S(2)}, u32[]{:S(2)}) %all-to-all-start.2) | async-done | bytes 1048608 | tf_op jit(solution)/shard_map/all_to_all | solution.py:89
  643.2 8.4 %convert_reduce_fusion = f32[128,1536]{1,0:T(8,128)S(1)} fusion(bf16[32,128,1536]{2,1,0:T(8,128)(2,1)} %bitcast.33, bf16[32,128,128]{2,1,0:T(8,128)(2,1)} %all-to-all-done.2), kind=kOutput, calls=%fused_computation.2 | convolution fusion | flops 1629290496 | bytes 14417920 | tf_op jit(solution)/shard_map/rgk,gkd->grd/dot_general | solution.py:92
  651.6 0.0 copy-start.2
  651.6 0.3 multiply_reduce_fusion
  652.0 0.1 multiply_convert_fusion
  652.1 1.2 copy-done.2
  653.3 1.1 fusion.86
  654.4 0.2 copy-done.5
  654.6 0.6 fusion.85
  655.2 0.7 copy-done.8
  655.8 1.0 convolution_convert_fusion.3
  656.9 0.1 subtract_convert_fusion
  656.9 0.7 subtract_convert_fusion.2
  657.6 1.6 copy.31
  659.2 0.7 pad_maximum_fusion.6
  659.9 2.9 fusion.81
  662.9 1.8 convolution_convert_fusion.1
  664.6 1.4 fusion.3
  (46 shorter events, 0.1 us)
Async XLA Ops:
  0.0 314.6 %copy-start = (bf16[768,1536]{1,0:T(8,128)(2,1)S(1)}, bf16[768,1536]{1,0:T(8,128)(2,1)}, u32[]{:S(2)}) copy-start(bf16[768,1536]{1,0:T(8,128)(2,1)} %param.23) | copy-start | bytes 7077892
  7.0 10.4 %copy-start.7 = (bf16[1,2,256,384]{3,2,1,0:T(8,128)(2,1)S(1)}, bf16[1,2,256,384]{3,2,1,0:T(8,128)(2,1)}, u32[]{:S(2)}) copy-start(bf16[1,2,256,384]{3,2,1,0:T(8,128)(2,1)} %param.15) | copy-start | bytes 1179652
  7.1 301.5 %all-to-all-start = ((bf16[32,128,1536]{2,1,0:T(8,128)(2,1)}), bf16[32,128,1536]{2,1,0:T(8,128)(2,1)}, u32[]{:S(2)}, u32[]{:S(2)}) async-start(bf16[32,128,1536]{2,1,0:T(8,128)(2,1)} %broadcast_in_dim.20), calls=%async_computation | async-start | bytes 25165824 | tf_op jit(solution)/shard_map/all_to_all | solution.py:153
  17.4 222.7 %collective-permute-start = (bf16[2,256,384]{2,1,0:T(8,128)(2,1)S(1)}, bf16[2,256,384]{2,1,0:T(8,128)(2,1)S(1)}, u32[]{:S(2)}, u32[]{:S(2)}) collective-permute-start(bf16[2,256,384]{2,1,0:T(8,128)(2,1)S(1)} %bitcast.159), channel_id=1, source_target_pairs={{0,128},{32,160},{64,192},{96,224},{128,0},{160,32},{192,64},{224,... | collective-permute-start | bytes 1179656 | tf_op jit(solution)/shard_map/ppermute | solution.py:110
  20.3 214.4 %collective-permute-start.1 = (s32[1]{0:T(128)}, s32[1]{0:T(128)}, u32[]{:S(2)}, u32[]{:S(2)}) collective-permute-start(s32[1]{0:T(128)} %param.17), channel_id=1, source_target_pairs={{0,32},{32,0},{64,96},{96,64},{128,160},{160,128},{192,224},{224,1... | collective-permute-start | bytes 20 | tf_op jit(solution)/shard_map/ppermute | solution.py:110
  25.2 5.0 copy-start.1
  25.2 5.2 copy-start.16
  235.4 2.8 collective-permute-start.2
  240.1 2.3 copy-start.20
  241.2 17.5 %collective-permute-start.3 = (bf16[2,2,256,384]{3,2,1,0:T(8,128)(2,1)}, bf16[2,2,256,384]{3,2,1,0:T(8,128)(2,1)}, u32[]{:S(2)}, u32[]{:S(2)}) collective-permute-start(bf16[2,2,256,384]{3,2,1,0:T(8,128)(2,1)} %pad_maximum_fusion), channel_id=1, source_target_pairs={{0,64},{32,96},{64,0},{96,32},{128,192},{160,224},{192,128},{224,1... | collective-permute-start | bytes 2359304 | tf_op jit(solution)/shard_map/ppermute | solution.py:110
  245.7 4.2 copy-start.6
  260.4 12.1 %collective-permute-start.4 = (bf16[2,256,384]{2,1,0:T(8,128)(2,1)}, bf16[2,256,384]{2,1,0:T(8,128)(2,1)}, u32[]{:S(2)}, u32[]{:S(2)}) collective-permute-start(bf16[2,256,384]{2,1,0:T(8,128)(2,1)} %fusion.28), channel_id=1, source_target_pairs={{0,32},{32,0},{64,96},{96,64},{128,160},{160,128},{192,224},{224,1... | collective-permute-start | bytes 1179656 | tf_op jit(solution)/shard_map/ppermute | solution.py:110
  274.5 35.5 %copy-start.17 = (bf16[128,4,48]{0,2,1:T(8,128)(2,1)S(1)}, bf16[128,4,48]{0,2,1:T(8,128)(2,1)}, u32[]{:S(2)}) copy-start(bf16[128,4,48]{0,2,1:T(8,128)(2,1)} %get-tuple-element.21) | copy-start | bytes 147460
  274.5 35.5 %copy-start.18 = (bf16[128,4,48]{0,2,1:T(8,128)(2,1)S(1)}, bf16[128,4,48]{0,2,1:T(8,128)(2,1)}, u32[]{:S(2)}) copy-start(bf16[128,4,48]{0,2,1:T(8,128)(2,1)} %get-tuple-element.22) | copy-start | bytes 147460
  309.8 3.1 copy-start.14
  310.0 2.9 copy-start.12
  310.0 2.9 copy-start.15
  314.6 1.5 copy-start.19
  315.2 0.9 copy-start.3
  322.1 280.3 %copy-start.11 = (bf16[1536,128]{1,0:T(8,128)(2,1)S(1)}, bf16[1536,128]{1,0:T(8,128)(2,1)}, u32[]{:S(2)}) copy-start(bf16[1536,128]{1,0:T(8,128)(2,1)} %param.25) | copy-start | bytes 1179652
  602.4 3.5 copy-start.21
  610.5 4.8 copy-start.22
  610.5 32.7 %all-to-all-start.2 = ((bf16[32,128,128]{2,1,0:T(8,128)(2,1)}), bf16[32,128,128]{2,1,0:T(8,128)(2,1)}, u32[]{:S(2)}, u32[]{:S(2)}) async-start(bf16[32,128,128]{2,1,0:T(8,128)(2,1)} %bitcast.161), calls=%async_computation.2 | async-start | bytes 2097152 | tf_op jit(solution)/shard_map/all_to_all | solution.py:89
  643.2 8.4 %copy-start.4 = (f32[128,1536]{1,0:T(8,128)S(1)}, f32[128,1536]{1,0:T(8,128)}, u32[]{:S(2)}) copy-start(f32[128,1536]{1,0:T(8,128)} %copy-done.3) | copy-start | bytes 2359300
  651.6 1.7 copy-start.2
  653.3 1.3 copy-start.5
  654.6 1.3 copy-start.8
  654.6 2.3 copy-start.9
  654.6 2.3 copy-start.10
  659.9 2.9 copy-start.13
